TPU v7x, 32 devices: a whole 2x2x4 slice. The times are simulated.
32 devices in a mesh: seq: 8 (over y, x, core), panel: 4 (over z).
Axes of the slice: x: 2, y: 2, z: 4, core: 2. Of those that a mesh axis runs over, the one named last changes fastest.
Arguments:
- tokens: bfloat16 [2048, 1024], P('seq', 'panel'), may hold values from -6 to 6
- cotangent: bfloat16 [2048, 1024], P('seq', 'panel'), may hold values from -6 to 6
- in_weight: bfloat16 [3, 1024, 1024], P(None, None, 'panel'), may hold values from -0.1875 to 0.1875
- short_kernel: float32 [3, 3, 1024], P(None, None, 'panel'), may hold values from -1 to 1
- skip_gain: float32 [1024], P('panel'), may hold values from 0.5 to 1.5
- long_filter: float32 [2048, 1024], P('seq', 'panel'), may hold values from -1.25 to 1.25
- out_weight: bfloat16 [1024, 1024], P('panel'), may hold values from -0.1875 to 0.1875
Outputs:
- block_out: bfloat16 [2048, 1024], P('seq', 'panel')
- token_grad: bfloat16 [2048, 1024], P('seq', 'panel')
All inputs are finite; a program needn't handle non-finite values.
Results may differ from a plain program's by a relative error of at most 0.007.
Values may be sent and summed in bfloat16 or wider, within the bound.
No kernel may reach another device: no remote copies, remote signals or barrier semaphores. Data moves between devices by JAX's collectives and lax.ppermute only.
A program may use at most 64 MiB of HBM per device.

v0:
```python
import math
import jax
import jax.numpy as jnp
import numpy as np
from jax import lax
from jax.sharding import PartitionSpec as P

HIGHEST = lax.Precision.HIGHEST
STAGE_A_PRECISION = lax.Precision.HIGH
STAGE_B_PRECISION = lax.Precision.HIGH
WIRE = jnp.bfloat16


def shifted(value, axis, steps):
    count = lax.axis_size(axis)
    initial, last = (max(0, -steps), min(count, count - steps))
    return lax.ppermute(value, axis, [(source, source + steps) for source in range(initial, last)])


def panel_parts(value):
    count = lax.axis_size("panel")
    me = lax.axis_index("panel")
    parts = [(value, me)]
    for k in range(1, count):
        moved = lax.ppermute(value, "panel", [(i, (i + k) % count) for i in range(count)])
        parts.append((moved, (me + count - k) % count))
    return parts


def panel_reduce_scatter(block_of):
    count = lax.axis_size("panel")
    me = lax.axis_index("panel")
    total = block_of(me)
    for k in range(1, count):
        sent = block_of((me + k) % count).astype(jnp.bfloat16)
        total = total + lax.ppermute(
            sent, "panel", [(i, (i + k) % count) for i in range(count)]
        ).astype(jnp.float32)
    return total.astype(jnp.bfloat16)


def phase(numer, period):
    return 2.0 * math.pi / period * (numer % period).astype(jnp.float32)


def transform_tables(shard_count, row_count):
    length = shard_count * row_count
    branch = jnp.arange(2, dtype=jnp.int32)
    shard = jnp.arange(shard_count, dtype=jnp.int32)
    row = jnp.arange(row_count, dtype=jnp.int32)
    small_shard, small_row = (np.arange(shard_count), np.arange(row_count))
    small_branch = np.arange(2)
    theta = (
        -2.0
        * math.pi
        / (2 * shard_count)
        * (
            (
                (2 * small_shard[:, None] * small_shard[None, :])[None]
                + small_branch[:, None, None] * small_shard[None, None, :]
            )
            % (2 * shard_count)
        )
    )
    stage_a_np = np.stack([np.cos(theta), np.sin(theta)], axis=1)
    stage_a = jnp.asarray(stage_a_np, dtype=jnp.float32)
    phi = (
        -2.0
        * math.pi
        / (2 * length)
        * (
            (
                (2 * small_shard[:, None] * small_row[None, :])[None]
                + small_branch[:, None, None] * small_row[None, :][None]
            )
            % (2 * length)
        )
    )
    twiddle = (jnp.asarray(np.cos(phi), jnp.float32), jnp.asarray(np.sin(phi), jnp.float32))
    psi = -phase(row[:, None] * row[None, :], row_count)
    cos_b, sin_b = (jnp.cos(psi), jnp.sin(psi))
    stage_b = jnp.stack([jnp.stack([cos_b, sin_b], axis=1), jnp.stack([-sin_b, cos_b], axis=1)])
    stage_a_inv = jnp.asarray(stage_a_np * (0.5 / length), dtype=jnp.float32)
    return (stage_a, twiddle, stage_b, stage_a_inv)


def complex_scale(value, cos_part, sin_part, axis):
    real_part = lax.index_in_dim(value, 0, axis, keepdims=False)
    imag_part = lax.index_in_dim(value, 1, axis, keepdims=False)
    return jnp.stack(
        [real_part * cos_part - imag_part * sin_part, real_part * sin_part + imag_part * cos_part],
        axis=axis,
    )


def to_columns(rows, wire=jnp.float32):
    shard_count = lax.axis_size("seq")
    batch, row_count, _ = rows.shape
    columns = lax.all_to_all(
        jnp.swapaxes(rows, 1, 2).astype(wire), "seq", split_axis=1, concat_axis=2, tiled=True
    ).astype(jnp.float32)
    return columns.reshape(batch, columns.shape[1], shard_count, row_count)


def to_rows(columns, wire=jnp.float32):
    batch, chan_count, shard_count, row_count = columns.shape
    rows = lax.all_to_all(
        columns.astype(wire), "seq", split_axis=2, concat_axis=1, tiled=True
    ).astype(jnp.float32)
    return jnp.swapaxes(rows.reshape(batch, shard_count * chan_count, row_count), 1, 2)


def forward_spectrum(columns, tables):
    stage_a, twiddle, stage_b, _ = tables
    spread = jnp.einsum("erkp,bcpm->bcerkm", stage_a, columns, precision=STAGE_A_PRECISION)
    spread = complex_scale(spread, twiddle[0], twiddle[1], 3)
    return jnp.einsum("bcerkm,rmsq->bceskq", spread, stage_b, precision=STAGE_B_PRECISION)


def inverse_spectrum(spectrum, tables):
    _, twiddle, stage_b, stage_a_inv = tables
    spread = jnp.einsum("bceskq,rmsq->bcerkm", spectrum, stage_b, precision=STAGE_B_PRECISION)
    spread = complex_scale(spread, twiddle[0], -twiddle[1], 3)
    return jnp.einsum("erkp,bcerkm->bcpm", stage_a_inv, spread, precision=STAGE_A_PRECISION)


def local(tokens, cotangent, in_weight, short_kernel, skip_gain, long_filter, out_weight):
    row_count = tokens.shape[0]
    tap_count = short_kernel.shape[0]
    shard_count = lax.axis_size("seq")
    tables = transform_tables(shard_count, row_count)
    filt_spec = forward_spectrum(to_columns(long_filter[None]), tables)
    width = tokens.shape[1]
    projected = 0.0
    for part, source in panel_parts(tokens):
        projected = projected + jnp.einsum(
            "td,jdc->jtc",
            part,
            lax.dynamic_slice_in_dim(in_weight, source * width, width, axis=1),
            preferred_element_type=jnp.float32,
        )
    grad_gated = 0.0
    for part, source in panel_parts(cotangent):
        grad_gated = grad_gated + lax.dot_general(
            part,
            lax.dynamic_slice_in_dim(out_weight, source * width, width, axis=1),
            (((1,), (1,)), ((), ())),
            preferred_element_type=jnp.float32,
        )
    projected = projected.astype(jnp.bfloat16)
    before = shifted(projected[:, row_count - (tap_count - 1) :, :], "seq", 1)
    extended = jnp.concatenate([before, projected], axis=1).astype(jnp.float32)
    filtered = short_kernel[0][:, None, :] * extended[:, tap_count - 1 :, :]
    for tap_index in range(1, tap_count):
        filtered = (
            filtered
            + short_kernel[tap_index][:, None, :]
            * extended[:, tap_count - 1 - tap_index : tap_count - 1 - tap_index + row_count, :]
        )
    gate_out, gate_in, value_path = (filtered[0], filtered[1], filtered[2])
    signal = value_path * gate_in
    grad_state = grad_gated * gate_out
    spectra = forward_spectrum(to_columns(jnp.stack([signal, grad_state]), WIRE), tables)
    filt_real, filt_imag = (filt_spec[:, :, :, 0], filt_spec[:, :, :, 1])
    sig_real, sig_imag = (spectra[0:1, :, :, 0], spectra[0:1, :, :, 1])
    grad_real, grad_imag = (spectra[1:2, :, :, 0], spectra[1:2, :, :, 1])
    product = jnp.concatenate(
        [
            jnp.stack(
                [
                    sig_real * filt_real - sig_imag * filt_imag,
                    sig_real * filt_imag + sig_imag * filt_real,
                ],
                axis=3,
            ),
            jnp.stack(
                [
                    grad_real * filt_real + grad_imag * filt_imag,
                    grad_imag * filt_real - grad_real * filt_imag,
                ],
                axis=3,
            ),
        ]
    )
    convolved = to_rows(inverse_spectrum(product, tables), WIRE)
    conv_state = convolved[0] + skip_gain[None, :] * signal
    grad_signal = convolved[1] + skip_gain[None, :] * grad_state
    gated_state = (conv_state * gate_out).astype(jnp.bfloat16)
    block_out = panel_reduce_scatter(
        lambda dest: jnp.dot(
            gated_state,
            lax.dynamic_slice_in_dim(out_weight, dest * width, width, axis=1),
            preferred_element_type=jnp.float32,
        )
    )
    grad_gate_out = grad_gated * conv_state
    grad_value = grad_signal * gate_in
    grad_gate_in = grad_signal * value_path
    upstream = jnp.stack([grad_gate_out, grad_gate_in, grad_value])
    after_rim = shifted(upstream[:, : tap_count - 1, :], "seq", -1)
    widened = jnp.concatenate([upstream, after_rim], axis=1)
    grad_projected = short_kernel[0][:, None, :] * widened[:, :row_count, :]
    for tap_index in range(1, tap_count):
        grad_projected = (
            grad_projected
            + short_kernel[tap_index][:, None, :] * widened[:, tap_index : tap_index + row_count, :]
        )
    grad_projected = grad_projected.astype(jnp.bfloat16)
    token_grad = panel_reduce_scatter(
        lambda dest: jnp.einsum(
            "jtc,jdc->td",
            grad_projected,
            lax.dynamic_slice_in_dim(in_weight, dest * width, width, axis=1),
            preferred_element_type=jnp.float32,
        )
    )
    return (block_out, token_grad)


def solution(mesh):
    placed = (
        P("seq", "panel"),
        P("seq", "panel"),
        P(None, None, "panel"),
        P(None, None, "panel"),
        P("panel"),
        P("seq", "panel"),
        P("panel", None),
    )
    return jax.shard_map(
        local,
        mesh=mesh,
        in_specs=placed,
        out_specs=(P("seq", "panel"), P("seq", "panel")),
        check_vma=False,
    )
```

profile of v0, /device:TPU:9, one launch (start us, length us, event | category | flops | bytes accessed | tf_op | source)
XLA Modules:
  0.0 95.5 jit_solution(1160381794692749451)
XLA Ops:
  0.7 1.3 %collective-permute-start = (bf16[256,256]{1,0:T(8,128)(2,1)}, bf16[256,256]{1,0:T(8,128)(2,1)}, u32[]{:S(2)}, u32[]{:S(2)}) collective-permute-start(bf16[256,256]{1,0:T(8,128)(2,1)} %param.11), channel_id=1, source_target_pairs={{0,1},{1,2},{2,3},{3,0},{4,5},{5,6},{6,7},{7,4},{8,9},{9,10},{10,1... | collective-permute-start | bytes 393224 | tf_op jit(solution)/shard_map/ppermute | solution.py:25
  2.2 2.3 %collective-permute-start.1 = (bf16[256,256]{1,0:T(8,128)(2,1)}, bf16[256,256]{1,0:T(8,128)(2,1)}, u32[]{:S(2)}, u32[]{:S(2)}) collective-permute-start(bf16[256,256]{1,0:T(8,128)(2,1)} %param.11), channel_id=1, source_target_pairs={{0,2},{1,3},{2,0},{3,1},{4,6},{5,7},{6,4},{7,5},{8,10},{9,11},{10,... | collective-permute-start | bytes 393224 | tf_op jit(solution)/shard_map/ppermute | solution.py:25
  4.5 1.0 %collective-permute-start.4 = (bf16[256,256]{1,0:T(8,128)(2,1)}, bf16[256,256]{1,0:T(8,128)(2,1)}, u32[]{:S(2)}, u32[]{:S(2)}) collective-permute-start(bf16[256,256]{1,0:T(8,128)(2,1)} %param.12), channel_id=1, source_target_pairs={{0,1},{1,2},{2,3},{3,0},{4,5},{5,6},{6,7},{7,4},{8,9},{9,10},{10,1... | collective-permute-start | bytes 393224 | tf_op jit(solution)/shard_map/ppermute | solution.py:25
  5.5 0.5 collective-permute-start.6
  6.0 1.8 %copy.64 = f32[1,256,256]{1,0,2:T(1,128)} copy(f32[1,256,256]{2,1,0:T(8,128)} %bitcast.216) | data formatting | bytes 524288 | tf_op jit(solution)/shard_map/broadcast_in_dim | solution.py:132
  7.7 5.8 %all-to-all-start.1 = ((f32[1,256,256]{2,0,1:T(1,128)}), f32[1,256,256]{2,0,1:T(1,128)S(1)}, u32[]{:S(2)}, u32[]{:S(2)}) async-start(f32[1,256,256]{2,0,1:T(1,128)} %bitcast.34), calls=%async_computation.1 | async-start | bytes 524288 | tf_op jit(solution)/shard_map/all_to_all | solution.py:99
  13.5 1.0 %fusion.88 = f32[256,1,256]{2,0,1:T(8,128)S(1)} fusion(), kind=kLoop, calls=%fused_computation.124 | loop fusion | flops 1048576 | bytes 262144 | tf_op jit(solution)/shard_map/neg | solution.py:82
  14.5 1.0 %fusion.86 = (f32[256,1,256]{2,0,1:T(8,128)S(1)}, f32[256,1,256]{2,0,1:T(8,128)S(1)}) fusion(), kind=kLoop, calls=%fused_computation.122 | loop fusion | flops 983040 | bytes 524288 | tf_op jit(solution)/shard_map/sin | solution.py:81
  15.6 0.7 slice_bitcast_fusion.5
  16.3 1.9 %fusion.98 = f32[256,256]{0,1:T(8,128)} fusion(bf16[256,256]{1,0:T(8,128)(2,1)} %param.12, bf16[256,1024]{1,0:T(8,128)(2,1)} %param.17, s32[]{:T(128)S(6)} %select_n.85), kind=kOutput, calls=%fused_computation.134 | convolution fusion | flops 33554432 | bytes 524292 | tf_op jit(solution)/shard_map/dot_general | solution.py:144
  18.5 1.1 %maximum_bitcast_fusion.2 = (f32[1,256,2,256]{3,1,0,2:T(8,128)}, f32[1,256,2,256]{3,1,0,2:T(8,128)}) fusion(f32[256,1,256]{2,0,1:T(8,128)S(1)} %get-tuple-element.25, f32[256,1,256]{2,0,1:T(8,128)S(1)} %get-tuple-element.26, f32[256,1,256]{2,0,1:T(8,128)S(1)} %fusion.88), kind=kLoop, calls=%fused_computation.62 | loop fusion | flops 262144 | bytes 1835008 | tf_op jit(solution)/shard_map/stack | solution.py:82
  19.6 0.5 collective-permute-start.5
  20.1 1.2 %convolution_add_fusion.1 = f32[3,256,256]{1,2,0:T(8,128)S(1)} fusion(f32[3,256,256]{1,2,0:T(8,128)S(1)} %fusion.51, bf16[3,1024,256]{2,1,0:T(8,128)(2,1)S(1)} %copy-done, s32[]{:T(128)S(6)} %select_n.87, bf16[256,256]{1,0:T(8,128)(2,1)} %collective-permute-done), kind=kOutput, calls=%fused_computation.19 | convolution fusion | flops 100859904 | bytes 2097156 | tf_op jit(solution)/shard_map/td,jdc->jtc/dot_general | solution.py:136
  21.3 1.2 %fusion.44 = f32[3,256,256]{1,2,0:T(8,128)S(1)} fusion(bf16[3,1024,256]{2,1,0:T(8,128)(2,1)S(1)} %copy-done, s32[]{:T(128)S(6)} %select_n.91, bf16[256,256]{1,0:T(8,128)(2,1)} %collective-permute-done.2), kind=kOutput, calls=%fused_computation.75 | convolution fusion | flops 100663296 | bytes 1310724 | tf_op jit(solution)/shard_map/td,jdc->jtc/dot_general | solution.py:136
  22.6 1.2 %fusion.21 = bf16[3,256,256]{2,1,0:T(8,128)(2,1)S(1)} fusion(f32[3,256,256]{1,2,0:T(8,128)S(1)} %fusion.44, f32[3,256,256]{1,2,0:T(8,128)S(1)} %convolution_add_fusion.1, bf16[3,1024,256]{2,1,0:T(8,128)(2,1)S(1)} %copy-done, s32[]{:T(128)S(6)} %select_n.89, bf16[256,256]{1,0:T(8,128)(2,1)} %collective-permute-done.1), kind=kOutput, calls=%fused_computation.22 | convolution fusion | flops 101253120 | bytes 2490372 | tf_op jit(solution)/shard_map/td,jdc->jtc/dot_general | solution.py:136
  23.8 3.8 %collective-permute-start.3 = (bf16[3,2,256]{2,1,0:T(2,128)(2,1)S(1)}, bf16[3,2,256]{2,1,0:T(2,128)(2,1)S(1)}, u32[]{:S(2)}, u32[]{:S(2)}) collective-permute-start(bf16[3,2,256]{2,1,0:T(2,128)(2,1)S(1)} %slice.111), channel_id=1, source_target_pairs={{0,4},{4,8},{8,12},{12,16},{16,20},{20,24},{24,28},{1,5},{5,9},{9,... | collective-permute-start | bytes 9224 | tf_op jit(solution)/shard_map/ppermute | solution.py:17
  27.6 1.1 %convolution_add_fusion.3 = f32[256,256]{0,1:T(8,128)S(1)} fusion(f32[256,256]{0,1:T(8,128)S(1)} %copy-done.9, bf16[256,256]{1,0:T(8,128)(2,1)} %collective-permute-done.4, bf16[256,1024]{1,0:T(8,128)(2,1)S(1)} %copy-done.7, s32[]{:T(128)S(6)} %select_n.87), kind=kOutput, calls=%fused_computation.31 | convolution fusion | flops 33619968 | bytes 786436 | tf_op jit(solution)/shard_map/dot_general | solution.py:144
  28.8 1.1 %fusion.90 = f32[256,256]{0,1:T(8,128)S(1)} fusion(bf16[256,256]{1,0:T(8,128)(2,1)} %collective-permute-done.6, bf16[256,1024]{1,0:T(8,128)(2,1)S(1)} %copy-done.7, s32[]{:T(128)S(6)} %select_n.91), kind=kOutput, calls=%fused_computation.126 | convolution fusion | flops 33554432 | bytes 524292 | tf_op jit(solution)/shard_map/dot_general | solution.py:144
  31.1 0.9 copy.34
  31.9 4.2 %all-to-all-start = ((bf16[2,256,256]{2,0,1:T(2,128)(2,1)}), bf16[2,256,256]{2,0,1:T(2,128)(2,1)}, u32[]{:S(2)}, u32[]{:S(2)}) async-start(bf16[2,256,256]{2,0,1:T(2,128)(2,1)} %copy.34), calls=%async_computation | async-start | bytes 524288 | tf_op jit(solution)/shard_map/all_to_all | solution.py:99
  36.1 0.6 convolution_bitcast_fusion.2
  37.0 0.8 copy-done.1
  37.9 1.1 %convolution_bitcast_fusion.1 = f32[1,32,2,2,8,256]{5,1,4,2,0,3:T(8,128)S(1)} fusion(f32[32,2,2,8,256]{4,3,0,2,1:T(8,128)S(1)} %maximum_bitcast_fusion.1, f32[1,256,2,256]{3,1,0,2:T(8,128)S(1)} %copy-done.3, f32[1,256,2,256]{3,1,0,2:T(8,128)S(1)} %copy-done.1), kind=kOutput, calls=%fused_computation.15 | convolution fusion | flops 805568512 | bytes 3145728 | tf_op jit(solution)/shard_map/bcerkm,rmsq->bceskq/dot_general | solution.py:117
  39.1 2.4 %all-to-all-done = bf16[2,256,256]{2,0,1:T(2,128)(2,1)} async-done(((bf16[2,256,256]{2,0,1:T(2,128)(2,1)}), bf16[2,256,256]{2,0,1:T(2,128)(2,1)}, u32[]{:S(2)}, u32[]{:S(2)}) %all-to-all-start) | async-done | bytes 262176 | tf_op jit(solution)/shard_map/all_to_all | solution.py:99
  41.5 1.7 %convolution_bitcast_fusion = f32[2,32,2,2,8,256]{5,4,3,2,1,0:T(8,128)S(1)} fusion(f32[2,2,8,8,1,1]{3,2,1,0,5,4:T(8,128)S(1)} %copy-done.15, bf16[2,8,32,256]{3,0,2,1:T(2,128)(2,1)} %bitcast.18), kind=kOutput, calls=%fused_computation.14 | convolution fusion | flops 25165824 | bytes 2360320 | tf_op jit(solution)/shard_map/erkp,bcpm->bcerkm/dot_general | solution.py:115
  43.7 0.8 copy-done.2
  44.7 2.7 %fusion.10 = f32[2,32,2,2,8,256]{5,1,4,2,0,3:T(8,128)S(1)} fusion(f32[2,32,2,2,8,256]{5,4,3,2,1,0:T(8,128)S(1)} %pad_maximum_fusion, f32[1,256,2,256]{3,1,0,2:T(8,128)S(1)} %copy-done.4, f32[1,256,2,256]{3,1,0,2:T(8,128)S(1)} %copy-done.2), kind=kOutput, calls=%fused_computation.12 | convolution fusion | flops 1610874880 | bytes 5242880 | tf_op jit(solution)/shard_map/bcerkm,rmsq->bceskq/dot_general | solution.py:117
  47.3 0.5 multiply_subtract_fusion.3
  48.1 2.7 %fusion.13 = f32[2,32,2,2,8,256]{5,4,3,2,1,0:T(8,128)S(1)} fusion(f32[2,32,2,2,8,256,1]{5,1,4,2,0,3,6:T(8,128)S(1)} %maximum_bitcast_fusion, f32[1,256,2,256]{3,1,0,2:T(8,128)S(1)} %copy-done.4, f32[1,256,2,256]{3,1,0,2:T(8,128)S(1)} %copy-done.2), kind=kOutput, calls=%fused_computation.13 | convolution fusion | flops 1610874880 | bytes 5242880 | tf_op jit(solution)/shard_map/bceskq,rmsq->bcerkm/dot_general | solution.py:122
  51.1 0.4 copy-done.13
  51.5 0.7 fusion.27
  52.2 8.7 %all_to_all.39 = bf16[2,32,8,256]{3,1,0,2:T(8,128)(2,1)S(1)} all-to-all(bf16[2,32,8,256]{3,1,0,2:T(8,128)(2,1)S(1)} %copy.44), channel_id=1, replica_groups=mesh['seq'=8,'panel'=4] {'seq'}, dimensions={2} | all-to-all | bytes 524288 | tf_op jit(solution)/shard_map/all_to_all | solution.py:107
  60.9 0.8 bitcast_convert_fusion
  61.8 1.2 %copy.46 = f32[2,256,256]{1,2,0:T(8,128)S(1)} copy(f32[2,256,256]{2,1,0:T(8,128)} %bitcast.214) | data formatting | bytes 1048576 | tf_op jit(solution)/shard_map/transpose | solution.py:110
  63.2 0.8 copy-done.8
  64.5 3.1 %collective-permute-start.10 = (f32[3,2,256]{2,1,0:T(2,128)S(1)}, f32[3,2,256]{2,1,0:T(2,128)S(1)}, u32[]{:S(2)}, u32[]{:S(2)}) collective-permute-start(f32[3,2,256]{2,1,0:T(2,128)S(1)} %slice.132), channel_id=1, source_target_pairs={{4,0},{8,4},{12,8},{16,12},{20,16},{24,20},{28,24},{5,1},{9,5},{13... | collective-permute-start | bytes 18440 | tf_op jit(solution)/shard_map/ppermute | solution.py:17
  67.9 2.7 %collective-permute-start.7 = (bf16[256,256]{1,0:T(8,128)(2,1)S(1)}, bf16[256,256]{1,0:T(8,128)(2,1)S(1)}, u32[]{:S(2)}, u32[]{:S(2)}) collective-permute-start(bf16[256,256]{1,0:T(8,128)(2,1)S(1)} %convolution_convert_fusion.2), channel_id=1, source_target_pairs={{0,1},{1,2},{2,3},{3,0},{4,5},{5,6},{6,7},{7,4},{8,9},{9,10},{10,1... | collective-permute-start | bytes 393224 | tf_op jit(solution)/shard_map/ppermute | solution.py:36
  70.6 1.0 %collective-permute-start.8 = (bf16[256,256]{1,0:T(8,128)(2,1)S(1)}, bf16[256,256]{1,0:T(8,128)(2,1)S(1)}, u32[]{:S(2)}, u32[]{:S(2)}) collective-permute-start(bf16[256,256]{1,0:T(8,128)(2,1)S(1)} %convolution_convert_fusion.1), channel_id=1, source_target_pairs={{0,2},{1,3},{2,0},{3,1},{4,6},{5,7},{6,4},{7,5},{8,10},{9,11},{10,... | collective-permute-start | bytes 393224 | tf_op jit(solution)/shard_map/ppermute | solution.py:36
  72.8 1.2 %collective-permute-start.11 = (bf16[256,256]{1,0:T(8,128)(2,1)S(1)}, bf16[256,256]{1,0:T(8,128)(2,1)S(1)}, u32[]{:S(2)}, u32[]{:S(2)}) collective-permute-start(bf16[256,256]{1,0:T(8,128)(2,1)S(1)} %fusion.30), channel_id=1, source_target_pairs={{0,1},{1,2},{2,3},{3,0},{4,5},{5,6},{6,7},{7,4},{8,9},{9,10},{10,1... | collective-permute-start | bytes 393224 | tf_op jit(solution)/shard_map/ppermute | solution.py:36
  74.0 3.2 %collective-permute-start.12 = (bf16[256,256]{1,0:T(8,128)(2,1)S(1)}, bf16[256,256]{1,0:T(8,128)(2,1)S(1)}, u32[]{:S(2)}, u32[]{:S(2)}) collective-permute-start(bf16[256,256]{1,0:T(8,128)(2,1)S(1)} %fusion.31), channel_id=1, source_target_pairs={{0,2},{1,3},{2,0},{3,1},{4,6},{5,7},{6,4},{7,5},{8,10},{9,11},{10,... | collective-permute-start | bytes 393224 | tf_op jit(solution)/shard_map/ppermute | solution.py:36
  77.5 2.0 %collective-permute-done.7 = bf16[256,256]{1,0:T(8,128)(2,1)S(1)} collective-permute-done((bf16[256,256]{1,0:T(8,128)(2,1)S(1)}, bf16[256,256]{1,0:T(8,128)(2,1)S(1)}, u32[]{:S(2)}, u32[]{:S(2)}) %collective-permute-start.7) | collective-permute-done | bytes 131104 | tf_op jit(solution)/shard_map/ppermute | solution.py:36
  79.5 8.4 %collective-permute-done.8 = bf16[256,256]{1,0:T(8,128)(2,1)S(1)} collective-permute-done((bf16[256,256]{1,0:T(8,128)(2,1)S(1)}, bf16[256,256]{1,0:T(8,128)(2,1)S(1)}, u32[]{:S(2)}, u32[]{:S(2)}) %collective-permute-start.8) | collective-permute-done | bytes 131104 | tf_op jit(solution)/shard_map/ppermute | solution.py:36
  87.9 0.9 collective-permute-done.9
  88.8 0.9 add_convert_fusion
  89.7 1.0 %collective-permute-done.11 = bf16[256,256]{1,0:T(8,128)(2,1)S(1)} collective-permute-done((bf16[256,256]{1,0:T(8,128)(2,1)S(1)}, bf16[256,256]{1,0:T(8,128)(2,1)S(1)}, u32[]{:S(2)}, u32[]{:S(2)}) %collective-permute-start.11) | collective-permute-done | bytes 131104 | tf_op jit(solution)/shard_map/ppermute | solution.py:36
  90.7 2.7 %collective-permute-done.12 = bf16[256,256]{1,0:T(8,128)(2,1)S(1)} collective-permute-done((bf16[256,256]{1,0:T(8,128)(2,1)S(1)}, bf16[256,256]{1,0:T(8,128)(2,1)S(1)}, u32[]{:S(2)}, u32[]{:S(2)}) %collective-permute-start.12) | collective-permute-done | bytes 131104 | tf_op jit(solution)/shard_map/ppermute | solution.py:36
  93.5 1.0 %collective-permute-done.13 = bf16[256,256]{1,0:T(8,128)(2,1)S(1)} collective-permute-done((bf16[256,256]{1,0:T(8,128)(2,1)S(1)}, bf16[256,256]{1,0:T(8,128)(2,1)S(1)}, u32[]{:S(2)}, u32[]{:S(2)}) %collective-permute-start.13) | collective-permute-done | bytes 131104 | tf_op jit(solution)/shard_map/ppermute | solution.py:36
  94.5 1.0 %fusion.62 = bf16[256,256]{1,0:T(8,128)(2,1)} fusion(bf16[3,256,256]{2,1,0:T(8,128)(2,1)S(1)} %fusion.39, bf16[3,1024,256]{2,1,0:T(8,128)(2,1)S(1)} %copy-done, s32[]{:T(128)S(6)} %select_n.85, bf16[256,256]{1,0:T(8,128)(2,1)S(1)} %collective-permute-done.13, bf16[256,256]{1,0:T(8,128)(2,1)S(1)} %collective-permute-done.12, ...), kind=kOutput, calls=%fused_computation.87 | convolution fusion | flops 101122048 | bytes 1310724 | tf_op jit(solution)/shard_map/jtc,jdc->td/dot_general | solution.py:210
  (72 shorter events, 5.5 us)
Async XLA Ops:
  0.6 17.6 %copy-start = (bf16[3,1024,256]{2,1,0:T(8,128)(2,1)S(1)}, bf16[3,1024,256]{2,1,0:T(8,128)(2,1)}, u32[]{:S(2)}) copy-start(bf16[3,1024,256]{2,1,0:T(8,128)(2,1)} %param.13) | copy-start | bytes 4718596
  0.6 17.6 %copy-start.11 = (bf16[256,256]{1,0:T(8,128)(2,1)S(1)}, bf16[256,256]{1,0:T(8,128)(2,1)}, u32[]{:S(2)}) copy-start(bf16[256,256]{1,0:T(8,128)(2,1)} %param.11) | copy-start | bytes 393220
  0.7 18.9 %collective-permute-start = (bf16[256,256]{1,0:T(8,128)(2,1)}, bf16[256,256]{1,0:T(8,128)(2,1)}, u32[]{:S(2)}, u32[]{:S(2)}) collective-permute-start(bf16[256,256]{1,0:T(8,128)(2,1)} %param.11), channel_id=1, source_target_pairs={{0,1},{1,2},{2,3},{3,0},{4,5},{5,6},{6,7},{7,4},{8,9},{9,10},{10,1... | collective-permute-start | bytes 393224 | tf_op jit(solution)/shard_map/ppermute | solution.py:25
  2.0 19.3 %collective-permute-start.2 = (bf16[256,256]{1,0:T(8,128)(2,1)}, bf16[256,256]{1,0:T(8,128)(2,1)}, u32[]{:S(2)}, u32[]{:S(2)}) collective-permute-start(bf16[256,256]{1,0:T(8,128)(2,1)} %param.11), channel_id=1, source_target_pairs={{0,3},{1,0},{2,1},{3,2},{4,7},{5,4},{6,5},{7,6},{8,11},{9,8},{10,9... | collective-permute-start | bytes 393224 | tf_op jit(solution)/shard_map/ppermute | solution.py:25
  2.2 20.4 %collective-permute-start.1 = (bf16[256,256]{1,0:T(8,128)(2,1)}, bf16[256,256]{1,0:T(8,128)(2,1)}, u32[]{:S(2)}, u32[]{:S(2)}) collective-permute-start(bf16[256,256]{1,0:T(8,128)(2,1)} %param.11), channel_id=1, source_target_pairs={{0,2},{1,3},{2,0},{3,1},{4,6},{5,7},{6,4},{7,5},{8,10},{9,11},{10,... | collective-permute-start | bytes 393224 | tf_op jit(solution)/shard_map/ppermute | solution.py:25
  4.5 23.1 %collective-permute-start.4 = (bf16[256,256]{1,0:T(8,128)(2,1)}, bf16[256,256]{1,0:T(8,128)(2,1)}, u32[]{:S(2)}, u32[]{:S(2)}) collective-permute-start(bf16[256,256]{1,0:T(8,128)(2,1)} %param.12), channel_id=1, source_target_pairs={{0,1},{1,2},{2,3},{3,0},{4,5},{5,6},{6,7},{7,4},{8,9},{9,10},{10,1... | collective-permute-start | bytes 393224 | tf_op jit(solution)/shard_map/ppermute | solution.py:25
  5.5 23.3 %collective-permute-start.6 = (bf16[256,256]{1,0:T(8,128)(2,1)}, bf16[256,256]{1,0:T(8,128)(2,1)}, u32[]{:S(2)}, u32[]{:S(2)}) collective-permute-start(bf16[256,256]{1,0:T(8,128)(2,1)} %param.12), channel_id=1, source_target_pairs={{0,3},{1,0},{2,1},{3,2},{4,7},{5,4},{6,5},{7,6},{8,11},{9,8},{10,9... | collective-permute-start | bytes 393224 | tf_op jit(solution)/shard_map/ppermute | solution.py:25
  7.7 24.2 %all-to-all-start.1 = ((f32[1,256,256]{2,0,1:T(1,128)}), f32[1,256,256]{2,0,1:T(1,128)S(1)}, u32[]{:S(2)}, u32[]{:S(2)}) async-start(f32[1,256,256]{2,0,1:T(1,128)} %bitcast.34), calls=%async_computation.1 | async-start | bytes 524288 | tf_op jit(solution)/shard_map/all_to_all | solution.py:99
  19.6 10.3 %collective-permute-start.5 = (bf16[256,256]{1,0:T(8,128)(2,1)}, bf16[256,256]{1,0:T(8,128)(2,1)S(1)}, u32[]{:S(2)}, u32[]{:S(2)}) collective-permute-start(bf16[256,256]{1,0:T(8,128)(2,1)} %param.12), channel_id=1, source_target_pairs={{0,2},{1,3},{2,0},{3,1},{4,6},{5,7},{6,4},{7,5},{8,10},{9,11},{10,... | collective-permute-start | bytes 393224 | tf_op jit(solution)/shard_map/ppermute | solution.py:25
  21.3 6.3 %copy-start.7 = (bf16[256,1024]{1,0:T(8,128)(2,1)S(1)}, bf16[256,1024]{1,0:T(8,128)(2,1)}, u32[]{:S(2)}) copy-start(bf16[256,1024]{1,0:T(8,128)(2,1)} %param.17) | copy-start | bytes 1572868
  21.3 6.3 %copy-start.9 = (f32[256,256]{0,1:T(8,128)S(1)}, f32[256,256]{0,1:T(8,128)}, u32[]{:S(2)}) copy-start(f32[256,256]{0,1:T(8,128)} %fusion.98) | copy-start | bytes 786436
  23.8 6.4 %collective-permute-start.3 = (bf16[3,2,256]{2,1,0:T(2,128)(2,1)S(1)}, bf16[3,2,256]{2,1,0:T(2,128)(2,1)S(1)}, u32[]{:S(2)}, u32[]{:S(2)}) collective-permute-start(bf16[3,2,256]{2,1,0:T(2,128)(2,1)S(1)} %slice.111), channel_id=1, source_target_pairs={{0,4},{4,8},{8,12},{12,16},{16,20},{20,24},{24,28},{1,5},{5,9},{9,... | collective-permute-start | bytes 9224 | tf_op jit(solution)/shard_map/ppermute | solution.py:17
  30.2 0.7 copy-start.5
  30.9 5.2 %copy-start.16 = (f32[2,2,8,8,1]{3,2,4,1,0:T(8,128)S(1)}, f32[2,2,8,8,1]{3,2,4,1,0:T(8,128)}, u32[]{:S(2)}) copy-start(f32[2,2,8,8,1]{3,2,4,1,0:T(8,128)} %constant.93) | copy-start | bytes 3076
  31.0 5.8 %copy-start.10 = (f32[2,8,256]{2,1,0:T(8,128)S(1)}, f32[2,8,256]{2,1,0:T(8,128)}, u32[]{:S(2)}) copy-start(f32[2,8,256]{2,1,0:T(8,128)} %constant.88.clone) | copy-start | bytes 49156
  31.0 5.8 %copy-start.12 = (f32[2,8,256]{2,1,0:T(8,128)S(1)}, f32[2,8,256]{2,1,0:T(8,128)}, u32[]{:S(2)}) copy-start(f32[2,8,256]{2,1,0:T(8,128)} %constant.89.clone) | copy-start | bytes 49156
  31.9 9.6 %all-to-all-start = ((bf16[2,256,256]{2,0,1:T(2,128)(2,1)}), bf16[2,256,256]{2,0,1:T(2,128)(2,1)}, u32[]{:S(2)}, u32[]{:S(2)}) async-start(bf16[2,256,256]{2,0,1:T(2,128)(2,1)} %copy.34), calls=%async_computation | async-start | bytes 524288 | tf_op jit(solution)/shard_map/all_to_all | solution.py:99
  36.7 1.0 %copy-start.1 = (f32[1,256,2,256]{3,1,0,2:T(8,128)S(1)}, f32[1,256,2,256]{3,1,0,2:T(8,128)}, u32[]{:S(2)}) copy-start(f32[1,256,2,256]{3,1,0,2:T(8,128)} %get-tuple-element.20) | copy-start | bytes 1572868
  36.7 1.2 %copy-start.3 = (f32[1,256,2,256]{3,1,0,2:T(8,128)S(1)}, f32[1,256,2,256]{3,1,0,2:T(8,128)}, u32[]{:S(2)}) copy-start(f32[1,256,2,256]{3,1,0,2:T(8,128)} %get-tuple-element.21) | copy-start | bytes 1572868
  37.9 3.5 %copy-start.15 = (f32[2,2,8,8,1,1]{3,2,1,0,5,4:T(8,128)S(1)}, f32[2,2,8,8,1,1]{3,2,1,0,5,4:T(8,128)}, u32[]{:S(2)}) copy-start(f32[2,2,8,8,1,1]{3,2,1,0,5,4:T(8,128)} %constant.92) | copy-start | bytes 3076
  43.5 1.0 %copy-start.2 = (f32[1,256,2,256]{3,1,0,2:T(8,128)S(1)}, f32[1,256,2,256]{3,1,0,2:T(8,128)}, u32[]{:S(2)}) copy-start(f32[1,256,2,256]{3,1,0,2:T(8,128)} %get-tuple-element.20) | copy-start | bytes 1572868
  43.5 1.2 %copy-start.4 = (f32[1,256,2,256]{3,1,0,2:T(8,128)S(1)}, f32[1,256,2,256]{3,1,0,2:T(8,128)}, u32[]{:S(2)}) copy-start(f32[1,256,2,256]{3,1,0,2:T(8,128)} %get-tuple-element.21) | copy-start | bytes 1572868
  48.0 2.7 %copy-start.14 = (f32[2,8,256]{2,1,0:T(8,128)S(1)}, f32[2,8,256]{2,1,0:T(8,128)}, u32[]{:S(2)}) copy-start(f32[2,8,256]{2,1,0:T(8,128)} %constant.91) | copy-start | bytes 49156
  50.8 0.7 copy-start.13
  51.5 11.5 %copy-start.6 = (f32[256,256]{1,0:T(8,128)S(1)}, f32[256,256]{1,0:T(8,128)}, u32[]{:S(2)}) copy-start(f32[256,256]{1,0:T(8,128)} %copy-done.5) | copy-start | bytes 786436
  51.5 11.5 %copy-start.17 = (f32[256]{0:T(256)S(1)}, f32[256]{0:T(256)}, u32[]{:S(2)}) copy-start(f32[256]{0:T(256)} %param.15) | copy-start | bytes 3076
  63.0 1.0 %copy-start.8 = (bf16[256,1024]{1,0:T(8,128)(2,1)S(1)}, bf16[256,1024]{1,0:T(8,128)(2,1)}, u32[]{:S(2)}) copy-start(bf16[256,1024]{1,0:T(8,128)(2,1)} %param.17) | copy-start | bytes 1572868
  64.5 7.3 %collective-permute-start.10 = (f32[3,2,256]{2,1,0:T(2,128)S(1)}, f32[3,2,256]{2,1,0:T(2,128)S(1)}, u32[]{:S(2)}, u32[]{:S(2)}) collective-permute-start(f32[3,2,256]{2,1,0:T(2,128)S(1)} %slice.132), channel_id=1, source_target_pairs={{4,0},{8,4},{12,8},{16,12},{20,16},{24,20},{28,24},{5,1},{9,5},{13... | collective-permute-start | bytes 18440 | tf_op jit(solution)/shard_map/ppermute | solution.py:17
  67.9 11.6 %collective-permute-start.7 = (bf16[256,256]{1,0:T(8,128)(2,1)S(1)}, bf16[256,256]{1,0:T(8,128)(2,1)S(1)}, u32[]{:S(2)}, u32[]{:S(2)}) collective-permute-start(bf16[256,256]{1,0:T(8,128)(2,1)S(1)} %convolution_convert_fusion.2), channel_id=1, source_target_pairs={{0,1},{1,2},{2,3},{3,0},{4,5},{5,6},{6,7},{7,4},{8,9},{9,10},{10,1... | collective-permute-start | bytes 393224 | tf_op jit(solution)/shard_map/ppermute | solution.py:36
  70.6 17.4 %collective-permute-start.8 = (bf16[256,256]{1,0:T(8,128)(2,1)S(1)}, bf16[256,256]{1,0:T(8,128)(2,1)S(1)}, u32[]{:S(2)}, u32[]{:S(2)}) collective-permute-start(bf16[256,256]{1,0:T(8,128)(2,1)S(1)} %convolution_convert_fusion.1), channel_id=1, source_target_pairs={{0,2},{1,3},{2,0},{3,1},{4,6},{5,7},{6,4},{7,5},{8,10},{9,11},{10,... | collective-permute-start | bytes 393224 | tf_op jit(solution)/shard_map/ppermute | solution.py:36
  71.5 17.3 %collective-permute-start.9 = (bf16[256,256]{1,0:T(8,128)(2,1)S(1)}, bf16[256,256]{1,0:T(8,128)(2,1)S(1)}, u32[]{:S(2)}, u32[]{:S(2)}) collective-permute-start(bf16[256,256]{1,0:T(8,128)(2,1)S(1)} %convolution_convert_fusion), channel_id=1, source_target_pairs={{0,3},{1,0},{2,1},{3,2},{4,7},{5,4},{6,5},{7,6},{8,11},{9,8},{10,9... | collective-permute-start | bytes 393224 | tf_op jit(solution)/shard_map/ppermute | solution.py:36
  72.8 17.9 %collective-permute-start.11 = (bf16[256,256]{1,0:T(8,128)(2,1)S(1)}, bf16[256,256]{1,0:T(8,128)(2,1)S(1)}, u32[]{:S(2)}, u32[]{:S(2)}) collective-permute-start(bf16[256,256]{1,0:T(8,128)(2,1)S(1)} %fusion.30), channel_id=1, source_target_pairs={{0,1},{1,2},{2,3},{3,0},{4,5},{5,6},{6,7},{7,4},{8,9},{9,10},{10,1... | collective-permute-start | bytes 393224 | tf_op jit(solution)/shard_map/ppermute | solution.py:36
  74.0 19.4 %collective-permute-start.12 = (bf16[256,256]{1,0:T(8,128)(2,1)S(1)}, bf16[256,256]{1,0:T(8,128)(2,1)S(1)}, u32[]{:S(2)}, u32[]{:S(2)}) collective-permute-start(bf16[256,256]{1,0:T(8,128)(2,1)S(1)} %fusion.31), channel_id=1, source_target_pairs={{0,2},{1,3},{2,0},{3,1},{4,6},{5,7},{6,4},{7,5},{8,10},{9,11},{10,... | collective-permute-start | bytes 393224 | tf_op jit(solution)/shard_map/ppermute | solution.py:36
  79.5 15.0 %collective-permute-start.13 = (bf16[256,256]{1,0:T(8,128)(2,1)S(1)}, bf16[256,256]{1,0:T(8,128)(2,1)S(1)}, u32[]{:S(2)}, u32[]{:S(2)}) collective-permute-start(bf16[256,256]{1,0:T(8,128)(2,1)S(1)} %fusion.32), channel_id=1, source_target_pairs={{0,3},{1,0},{2,1},{3,2},{4,7},{5,4},{6,5},{7,6},{8,11},{9,8},{10,9... | collective-permute-start | bytes 393224 | tf_op jit(solution)/shard_map/ppermute | solution.py:36
where the time goes:
time: 96.3 us; the launch traced here: 95.5 us
  starting transfers between devices  31.1 us (32%)
  matrix products  21.1 us (22%)
  waiting for transfers between devices  18.5 us (19%)
  blocking collectives  8.7 us (9%)
  local copies, waits for them, and re-layouts  8.3 us (9%)
  other arithmetic  6.54 us (7%)
  between operations  1.23 us (1%)
    ppermute x6, waiting for transfers between devices, panel_reduce_scatter(): lax.ppermute(sent, 'panel', [(i, (i + k) % count) for i in range(count)])  16.1 us
    all_to_all x2, starting transfers between devices, to_columns(): lax.all_to_all(jnp.swapaxes(rows, 1, 2).astype(wire), 'seq', split_axis=1...  9.98 us
    all_to_all x1, blocking collectives, to_rows(): lax.all_to_all(columns.astype(wire), 'seq', split_axis=2, concat_axis=1,...  8.7 us
    ppermute x6, starting transfers between devices, panel_reduce_scatter(): lax.ppermute(sent, 'panel', [(i, (i + k) % count) for i in range(count)])  8.36 us
    ppermute x2, starting transfers between devices, shifted(): lax.ppermute(value, axis, [(source, source + steps) for source in range(i...  6.95 us
    ppermute x6, starting transfers between devices, panel_parts(): lax.ppermute(value, 'panel', [(i, (i + k) % count) for i in range(count)])  5.8 us
    dot_general x4, matrix products, local(): lax.dot_general(part, lax.dynamic_slice_in_dim(out_weight, source * width...  4.43 us
    dot_general x4, matrix products, local(): jnp.einsum('td,jdc->jtc', part, lax.dynamic_slice_in_dim(in_weight, sourc...  3.86 us
  transfers between devices with their start and end apart: 16, of which 7 were waited for; matrix products, arithmetic and copies ran while one was open for 20% of the time, Pallas kernels for 0%

commit v1 on v0

--- a/solution.py
+++ b/solution.py
@@ -9,6 +9,18 @@
 STAGE_A_PRECISION = lax.Precision.HIGH
 STAGE_B_PRECISION = lax.Precision.HIGH
 WIRE = jnp.bfloat16
+
+
+def sent_to_each(x, axis, split, join):
+    ways, here = (lax.axis_size(axis), lax.axis_index(axis))
+    width = x.shape[split] // ways
+    turned = jnp.roll(x, -here * width, axis=split)
+    got = [lax.slice_in_dim(turned, 0, width, axis=split)]
+    for far in range(1, ways):
+        sent = lax.slice_in_dim(turned, far * width, (far + 1) * width, axis=split)
+        got.append(lax.ppermute(sent, axis, [(d, (d + far) % ways) for d in range(ways)]))
+    line = jnp.concatenate(got[::-1], axis=join)
+    return jnp.roll(line, (here + 1) * got[0].shape[join], axis=join)
 
 
 def shifted(value, axis, steps):
@@ -96,9 +108,7 @@
 def to_columns(rows, wire=jnp.float32):
     shard_count = lax.axis_size("seq")
     batch, row_count, _ = rows.shape
-    columns = lax.all_to_all(
-        jnp.swapaxes(rows, 1, 2).astype(wire), "seq", split_axis=1, concat_axis=2, tiled=True
-    ).astype(jnp.float32)
+    columns = sent_to_each(jnp.swapaxes(rows, 1, 2).astype(wire), "seq", 1, 2).astype(jnp.float32)
     return columns.reshape(batch, columns.shape[1], shard_count, row_count)
 
 

time: 96.3 us -> 156 us (1.62)
  local copies, waits for them, and re-layouts: 8.3 us -> 37.6 us
  waiting for transfers between devices: 18.5 us -> 39.4 us
  starting transfers between devices: 31.1 us -> 38.9 us
  other arithmetic: 6.54 us -> 8.8 us
  matrix products: 21.1 us -> 19.2 us
    ppermute x0 -> x14, waiting for transfers between devices: none -> 23.4 us  [sent_to_each(): lax.ppermute(sent, axis, [(d, (d + far) % ways) for d in range(ways)])]
    unnamed x37 -> x89, local copies, waits for them, and re-layouts: 3.63 us -> 22.2 us
    ppermute x0 -> x14, starting transfers between devices: none -> 16.7 us  [sent_to_each(): lax.ppermute(sent, axis, [(d, (d + far) % ways) for d in range(ways)])]
    all_to_all x2 -> x0, starting transfers between devices: 9.98 us -> none  [to_columns(): lax.all_to_all(jnp.swapaxes(rows, 1, 2).astype(wire), 'seq', split_axis=1...]
    ppermute x0 -> x7, local copies, waits for them, and re-layouts: none -> 9.32 us  [sent_to_each(): lax.ppermute(sent, axis, [(d, (d + far) % ways) for d in range(ways)])]
    slice x0 -> x3, local copies, waits for them, and re-layouts: none -> 2.54 us  [the longest x2 1.86 us: sent_to_each(): got = [lax.slice_in_dim(turned, 0, width, axis=split)]]
    all_to_all x2 -> x0, waiting for transfers between devices: 2.4 us -> none  [to_columns(): lax.all_to_all(jnp.swapaxes(rows, 1, 2).astype(wire), 'seq', split_axis=1...]
    dot_general x4, matrix products: 4.43 us -> 2.55 us  [local(): lax.dot_general(part, lax.dynamic_slice_in_dim(out_weight, source * width...]
  transfers between devices with their start and end apart: 16 -> 28, of which waited for: 7 -> 14; matrix products, arithmetic and copies ran while one was open for 20% -> 22% of each run, Pallas kernels for 0% -> 0%
where the time goes in v1:
time: 156 us; the launch traced here: 154 us
  waiting for transfers between devices  39.4 us (25%)
  starting transfers between devices  38.9 us (25%)
  local copies, waits for them, and re-layouts  37.6 us (24%)
  matrix products  19.2 us (12%)
  other arithmetic  8.8 us (6%)
  blocking collectives  8.76 us (6%)
    ppermute x14, waiting for transfers between devices, sent_to_each(): lax.ppermute(sent, axis, [(d, (d + far) % ways) for d in range(ways)])  23.4 us
    unnamed x89, local copies, waits for them, and re-layouts  22.2 us
    ppermute x14, starting transfers between devices, sent_to_each(): lax.ppermute(sent, axis, [(d, (d + far) % ways) for d in range(ways)])  16.7 us
    ppermute x6, waiting for transfers between devices, panel_reduce_scatter(): lax.ppermute(sent, 'panel', [(i, (i + k) % count) for i in range(count)])  16 us
    ppermute x7, local copies, waits for them, and re-layouts, sent_to_each(): lax.ppermute(sent, axis, [(d, (d + far) % ways) for d in range(ways)])  9.32 us
    all_to_all x1, blocking collectives, to_rows(): lax.all_to_all(columns.astype(wire), 'seq', split_axis=2, concat_axis=1,...  8.76 us
    ppermute x6, starting transfers between devices, panel_reduce_scatter(): lax.ppermute(sent, 'panel', [(i, (i + k) % count) for i in range(count)])  8.37 us
    ppermute x2, starting transfers between devices, shifted(): lax.ppermute(value, axis, [(source, source + steps) for source in range(i...  7.55 us
  transfers between devices with their start and end apart: 28, of which 14 were waited for; matrix products, arithmetic and copies ran while one was open for 22% of the time, Pallas kernels for 0%

profile of v1, /device:TPU:9, one launch (start us, length us, event | category | flops | bytes accessed | tf_op | source)
XLA Modules:
  0.0 154.0 jit_solution(13058274525907756097)
XLA Ops:
  0.7 1.3 collective-permute-start
  2.2 2.3 %collective-permute-start.1 = (bf16[256,256]{1,0:T(8,128)(2,1)}, bf16[256,256]{1,0:T(8,128)(2,1)}, u32[]{:S(2)}, u32[]{:S(2)}) collective-permute-start(bf16[256,256]{1,0:T(8,128)(2,1)} %param.11), channel_id=1, source_target_pairs={{0,2},{1,3},{2,0},{3,1},{4,6},{5,7},{6,4},{7,5},{8,10},{9,11},{10,... | collective-permute-start | bytes 393224 | tf_op jit(solution)/shard_map/ppermute | solution.py:37
  7.4 1.5 collective-permute-start.14
  9.8 1.8 %fusion.86 = (f32[256,1,256]{2,0,1:T(8,128)}, f32[256,1,256]{2,0,1:T(8,128)}) fusion(), kind=kLoop, calls=%fused_computation.126 | loop fusion | flops 983040 | bytes 524288 | tf_op jit(solution)/shard_map/sin | solution.py:93
  13.5 2.2 %maximum_bitcast_fusion.2 = (f32[1,256,2,256]{3,1,0,2:T(8,128)}, f32[1,256,2,256]{3,1,0,2:T(8,128)}) fusion(f32[256,1,256]{2,0,1:T(8,128)} %get-tuple-element.40, f32[256,1,256]{2,0,1:T(8,128)} %get-tuple-element.41, f32[256,1,256]{2,0,1:T(8,128)S(1)} %fusion.88), kind=kLoop, calls=%fused_computation.62 | loop fusion | flops 262144 | bytes 1835008 | tf_op jit(solution)/shard_map/stack | solution.py:94
  15.7 2.4 %collective-permute-start.15 = (f32[1,32,256]{2,1,0:T(8,128)}, f32[1,32,256]{2,1,0:T(8,128)S(1)}, u32[]{:S(2)}, u32[]{:S(2)}) collective-permute-start(f32[1,32,256]{2,1,0:T(8,128)} %get-tuple-element.25), channel_id=1, source_target_pairs={{0,24},{4,28},{8,0},{12,4},{16,8},{20,12},{24,16},{28,20},{1,25},{... | collective-permute-start | bytes 98312 | tf_op jit(solution)/shard_map/ppermute | solution.py:21
  19.4 3.6 %collective-permute-start.16 = (f32[1,32,256]{2,1,0:T(8,128)}, f32[1,32,256]{2,1,0:T(8,128)S(1)}, u32[]{:S(2)}, u32[]{:S(2)}) collective-permute-start(f32[1,32,256]{2,1,0:T(8,128)} %get-tuple-element.24), channel_id=1, source_target_pairs={{0,20},{4,24},{8,28},{12,0},{16,4},{20,8},{24,12},{28,16},{1,21},{... | collective-permute-start | bytes 98312 | tf_op jit(solution)/shard_map/ppermute | solution.py:21
  23.0 1.3 collective-permute-done.16
  24.6 2.7 %collective-permute-done.17 = f32[1,32,256]{2,1,0:T(8,128)S(1)} collective-permute-done((f32[1,32,256]{2,1,0:T(8,128)}, f32[1,32,256]{2,1,0:T(8,128)S(1)}, u32[]{:S(2)}, u32[]{:S(2)}) %collective-permute-start.17) | collective-permute-done | bytes 32800 | tf_op jit(solution)/shard_map/ppermute | solution.py:21
  27.3 1.5 collective-permute-start.18
  28.9 4.5 %collective-permute-done.18 = f32[1,32,256]{2,1,0:T(8,128)S(1)} collective-permute-done((f32[1,32,256]{2,1,0:T(8,128)}, f32[1,32,256]{2,1,0:T(8,128)S(1)}, u32[]{:S(2)}, u32[]{:S(2)}) %collective-permute-start.18) | collective-permute-done | bytes 32800 | tf_op jit(solution)/shard_map/ppermute | solution.py:21
  33.4 3.9 %collective-permute-done.19 = f32[1,32,256]{2,1,0:T(8,128)S(1)} collective-permute-done((f32[1,32,256]{2,1,0:T(8,128)}, f32[1,32,256]{2,1,0:T(8,128)S(1)}, u32[]{:S(2)}, u32[]{:S(2)}) %collective-permute-start.19) | collective-permute-done | bytes 32800 | tf_op jit(solution)/shard_map/ppermute | solution.py:21
  38.3 1.3 collective-permute-done.20
  43.5 1.2 convolution_add_fusion.1
  44.7 1.2 fusion.44
  46.0 1.2 fusion.21
  47.2 4.4 %collective-permute-start.3 = (bf16[3,2,256]{2,1,0:T(2,128)(2,1)S(1)}, bf16[3,2,256]{2,1,0:T(2,128)(2,1)S(1)}, u32[]{:S(2)}, u32[]{:S(2)}) collective-permute-start(bf16[3,2,256]{2,1,0:T(2,128)(2,1)S(1)} %slice.175), channel_id=1, source_target_pairs={{0,4},{4,8},{8,12},{12,16},{16,20},{20,24},{24,28},{1,5},{5,9},{9,... | collective-permute-start | bytes 9224 | tf_op jit(solution)/shard_map/ppermute | solution.py:29
  55.5 1.5 convolution_bitcast_fusion.1
  57.7 1.7 %collective-permute-start.13 = (bf16[2,32,256]{1,2,0:T(8,128)(2,1)}, bf16[2,32,256]{1,2,0:T(8,128)(2,1)}, u32[]{:S(2)}, u32[]{:S(2)}) collective-permute-start(bf16[2,32,256]{1,2,0:T(8,128)(2,1)} %get-tuple-element.30), channel_id=1, source_target_pairs={{0,4},{4,8},{8,12},{12,16},{16,20},{20,24},{24,28},{28,0},{1,5},{5... | collective-permute-start | bytes 98312 | tf_op jit(solution)/shard_map/ppermute | solution.py:21
  59.4 2.4 %collective-permute-start.12 = (bf16[2,32,256]{1,2,0:T(8,128)(2,1)}, bf16[2,32,256]{1,2,0:T(8,128)(2,1)}, u32[]{:S(2)}, u32[]{:S(2)}) collective-permute-start(bf16[2,32,256]{1,2,0:T(8,128)(2,1)} %get-tuple-element.31), channel_id=1, source_target_pairs={{0,8},{4,12},{8,16},{12,20},{16,24},{20,28},{24,0},{28,4},{1,9},{5... | collective-permute-start | bytes 98312 | tf_op jit(solution)/shard_map/ppermute | solution.py:21
  61.9 1.5 collective-permute-start.8
  65.0 6.4 %collective-permute-done.8 = bf16[2,32,256]{1,2,0:T(8,128)(2,1)} collective-permute-done((bf16[2,32,256]{1,2,0:T(8,128)(2,1)}, bf16[2,32,256]{1,2,0:T(8,128)(2,1)}, u32[]{:S(2)}, u32[]{:S(2)}) %collective-permute-start.8) | collective-permute-done | bytes 32800 | tf_op jit(solution)/shard_map/ppermute | solution.py:21
  73.8 2.6 %collective-permute-done.9 = bf16[2,32,256]{1,2,0:T(8,128)(2,1)} collective-permute-done((bf16[2,32,256]{1,2,0:T(8,128)(2,1)}, bf16[2,32,256]{1,2,0:T(8,128)(2,1)}, u32[]{:S(2)}, u32[]{:S(2)}) %collective-permute-start.9) | collective-permute-done | bytes 32800 | tf_op jit(solution)/shard_map/ppermute | solution.py:21
  78.0 1.6 %copy.35 = bf16[2,32,256]{2,1,0:T(8,128)(2,1)} copy(bf16[2,32,256]{1,2,0:T(8,128)(2,1)} %collective-permute-done.10) | data formatting | bytes 65536 | tf_op jit(solution)/shard_map/ppermute | solution.py:21
  79.5 1.4 constant_dynamic-update-slice_fusion.12
  80.9 1.6 %copy.36 = bf16[2,32,256]{2,1,0:T(8,128)(2,1)} copy(bf16[2,32,256]{1,2,0:T(8,128)(2,1)} %collective-permute-done.11) | data formatting | bytes 65536 | tf_op jit(solution)/shard_map/ppermute | solution.py:21
  82.5 1.4 constant_dynamic-update-slice_fusion.11
  83.9 1.6 %copy.37 = bf16[2,32,256]{2,1,0:T(8,128)(2,1)} copy(bf16[2,32,256]{1,2,0:T(8,128)(2,1)} %collective-permute-done.12) | data formatting | bytes 65536 | tf_op jit(solution)/shard_map/ppermute | solution.py:21
  85.5 1.4 constant_dynamic-update-slice_fusion.10
  86.9 1.6 %copy.38 = bf16[2,32,256]{2,1,0:T(8,128)(2,1)} copy(bf16[2,32,256]{1,2,0:T(8,128)(2,1)} %collective-permute-done.13) | data formatting | bytes 65536 | tf_op jit(solution)/shard_map/ppermute | solution.py:21
  88.5 1.4 constant_dynamic-update-slice_fusion.9
  89.9 1.4 constant_dynamic-update-slice_fusion.8
  93.2 1.4 constant_dynamic-update-slice_fusion.4
  94.5 1.4 constant_dynamic-update-slice_fusion.3
  95.9 1.4 constant_dynamic-update-slice_fusion.2
  97.3 1.4 constant_dynamic-update-slice_fusion.1
  100.3 1.4 convolution_bitcast_fusion
  103.1 2.7 %fusion.10 = f32[2,32,2,2,8,256]{5,1,4,2,0,3:T(8,128)S(1)} fusion(f32[2,32,2,2,8,256]{5,4,3,2,1,0:T(8,128)S(1)} %pad_maximum_fusion, f32[1,256,2,256]{3,1,0,2:T(8,128)S(1)} %copy-done.4, f32[1,256,2,256]{3,1,0,2:T(8,128)S(1)} %copy-done.2), kind=kOutput, calls=%fused_computation.12 | convolution fusion | flops 1610874880 | bytes 5242880 | tf_op jit(solution)/shard_map/bcerkm,rmsq->bceskq/dot_general | solution.py:127
  106.6 2.7 %fusion.13 = f32[2,32,2,2,8,256]{5,4,3,2,1,0:T(8,128)S(1)} fusion(f32[2,32,2,2,8,256,1]{5,1,4,2,0,3,6:T(8,128)S(1)} %maximum_bitcast_fusion, f32[1,256,2,256]{3,1,0,2:T(8,128)S(1)} %copy-done.4, f32[1,256,2,256]{3,1,0,2:T(8,128)S(1)} %copy-done.2), kind=kOutput, calls=%fused_computation.13 | convolution fusion | flops 1610874880 | bytes 5242880 | tf_op jit(solution)/shard_map/bceskq,rmsq->bcerkm/dot_general | solution.py:132
  110.7 8.8 %all_to_all.4 = bf16[2,32,8,256]{3,1,0,2:T(8,128)(2,1)S(1)} all-to-all(bf16[2,32,8,256]{3,1,0,2:T(8,128)(2,1)S(1)} %copy.54), channel_id=1, replica_groups=mesh['seq'=8,'panel'=4] {'seq'}, dimensions={2} | all-to-all | bytes 524288 | tf_op jit(solution)/shard_map/all_to_all | solution.py:117
  120.3 1.2 copy.56
  123.1 3.1 %collective-permute-start.24 = (f32[3,2,256]{2,1,0:T(2,128)S(1)}, f32[3,2,256]{2,1,0:T(2,128)S(1)}, u32[]{:S(2)}, u32[]{:S(2)}) collective-permute-start(f32[3,2,256]{2,1,0:T(2,128)S(1)} %slice.212), channel_id=1, source_target_pairs={{4,0},{8,4},{12,8},{16,12},{20,16},{24,20},{28,24},{5,1},{9,5},{13... | collective-permute-start | bytes 18440 | tf_op jit(solution)/shard_map/ppermute | solution.py:29
  126.4 2.7 %collective-permute-start.21 = (bf16[256,256]{1,0:T(8,128)(2,1)S(1)}, bf16[256,256]{1,0:T(8,128)(2,1)S(1)}, u32[]{:S(2)}, u32[]{:S(2)}) collective-permute-start(bf16[256,256]{1,0:T(8,128)(2,1)S(1)} %convolution_convert_fusion.2), channel_id=1, source_target_pairs={{0,1},{1,2},{2,3},{3,0},{4,5},{5,6},{6,7},{7,4},{8,9},{9,10},{10,1... | collective-permute-start | bytes 393224 | tf_op jit(solution)/shard_map/ppermute | solution.py:48
  131.4 1.2 collective-permute-start.25
  132.6 3.2 %collective-permute-start.26 = (bf16[256,256]{1,0:T(8,128)(2,1)S(1)}, bf16[256,256]{1,0:T(8,128)(2,1)S(1)}, u32[]{:S(2)}, u32[]{:S(2)}) collective-permute-start(bf16[256,256]{1,0:T(8,128)(2,1)S(1)} %fusion.31), channel_id=1, source_target_pairs={{0,2},{1,3},{2,0},{3,1},{4,6},{5,7},{6,4},{7,5},{8,10},{9,11},{10,... | collective-permute-start | bytes 393224 | tf_op jit(solution)/shard_map/ppermute | solution.py:48
  136.1 1.9 %collective-permute-done.21 = bf16[256,256]{1,0:T(8,128)(2,1)S(1)} collective-permute-done((bf16[256,256]{1,0:T(8,128)(2,1)S(1)}, bf16[256,256]{1,0:T(8,128)(2,1)S(1)}, u32[]{:S(2)}, u32[]{:S(2)}) %collective-permute-start.21) | collective-permute-done | bytes 131104 | tf_op jit(solution)/shard_map/ppermute | solution.py:48
  138.1 8.4 %collective-permute-done.22 = bf16[256,256]{1,0:T(8,128)(2,1)S(1)} collective-permute-done((bf16[256,256]{1,0:T(8,128)(2,1)S(1)}, bf16[256,256]{1,0:T(8,128)(2,1)S(1)}, u32[]{:S(2)}, u32[]{:S(2)}) %collective-permute-start.22) | collective-permute-done | bytes 131104 | tf_op jit(solution)/shard_map/ppermute | solution.py:48
  149.3 2.7 %collective-permute-done.26 = bf16[256,256]{1,0:T(8,128)(2,1)S(1)} collective-permute-done((bf16[256,256]{1,0:T(8,128)(2,1)S(1)}, bf16[256,256]{1,0:T(8,128)(2,1)S(1)}, u32[]{:S(2)}, u32[]{:S(2)}) %collective-permute-start.26) | collective-permute-done | bytes 131104 | tf_op jit(solution)/shard_map/ppermute | solution.py:48
  (162 shorter events, 39.1 us)
Async XLA Ops:
  0.6 12.6 %copy-start = (bf16[3,1024,256]{2,1,0:T(8,128)(2,1)S(1)}, bf16[3,1024,256]{2,1,0:T(8,128)(2,1)}, u32[]{:S(2)}) copy-start(bf16[3,1024,256]{2,1,0:T(8,128)(2,1)} %param.13) | copy-start | bytes 4718596
  0.6 12.6 %copy-start.12 = (bf16[256,256]{1,0:T(8,128)(2,1)S(1)}, bf16[256,256]{1,0:T(8,128)(2,1)}, u32[]{:S(2)}) copy-start(bf16[256,256]{1,0:T(8,128)(2,1)} %param.11) | copy-start | bytes 393220
  0.7 11.6 %copy-start.13 = (bf16[256,256]{1,0:T(8,128)(2,1)S(1)}, bf16[256,256]{1,0:T(8,128)(2,1)}, u32[]{:S(2)}) copy-start(bf16[256,256]{1,0:T(8,128)(2,1)} %param.12) | copy-start | bytes 393220
  0.7 11.0 %copy-start.26 = (f32[3,3,256]{2,1,0:T(4,128)S(1)}, f32[3,3,256]{2,1,0:T(4,128)}, u32[]{:S(2)}) copy-start(f32[3,3,256]{2,1,0:T(4,128)} %param.14) | copy-start | bytes 27652
  0.7 11.6 %copy-start.7 = (bf16[256,1024]{1,0:T(8,128)(2,1)S(1)}, bf16[256,1024]{1,0:T(8,128)(2,1)}, u32[]{:S(2)}) copy-start(bf16[256,1024]{1,0:T(8,128)(2,1)} %param.17) | copy-start | bytes 1572868
  0.7 41.4 %collective-permute-start = (bf16[256,256]{1,0:T(8,128)(2,1)}, bf16[256,256]{1,0:T(8,128)(2,1)}, u32[]{:S(2)}, u32[]{:S(2)}) collective-permute-start(bf16[256,256]{1,0:T(8,128)(2,1)} %param.11), channel_id=1, source_target_pairs={{0,1},{1,2},{2,3},{3,0},{4,5},{5,6},{6,7},{7,4},{8,9},{9,10},{10,1... | collective-permute-start | bytes 393224 | tf_op jit(solution)/shard_map/ppermute | solution.py:37
  2.0 42.7 %collective-permute-start.2 = (bf16[256,256]{1,0:T(8,128)(2,1)}, bf16[256,256]{1,0:T(8,128)(2,1)}, u32[]{:S(2)}, u32[]{:S(2)}) collective-permute-start(bf16[256,256]{1,0:T(8,128)(2,1)} %param.11), channel_id=1, source_target_pairs={{0,3},{1,0},{2,1},{3,2},{4,7},{5,4},{6,5},{7,6},{8,11},{9,8},{10,9... | collective-permute-start | bytes 393224 | tf_op jit(solution)/shard_map/ppermute | solution.py:37
  2.2 43.8 %collective-permute-start.1 = (bf16[256,256]{1,0:T(8,128)(2,1)}, bf16[256,256]{1,0:T(8,128)(2,1)}, u32[]{:S(2)}, u32[]{:S(2)}) collective-permute-start(bf16[256,256]{1,0:T(8,128)(2,1)} %param.11), channel_id=1, source_target_pairs={{0,2},{1,3},{2,0},{3,1},{4,6},{5,7},{6,4},{7,5},{8,10},{9,11},{10,... | collective-permute-start | bytes 393224 | tf_op jit(solution)/shard_map/ppermute | solution.py:37
  4.5 47.1 %collective-permute-start.4 = (bf16[256,256]{1,0:T(8,128)(2,1)}, bf16[256,256]{1,0:T(8,128)(2,1)}, u32[]{:S(2)}, u32[]{:S(2)}) collective-permute-start(bf16[256,256]{1,0:T(8,128)(2,1)} %param.12), channel_id=1, source_target_pairs={{0,1},{1,2},{2,3},{3,0},{4,5},{5,6},{6,7},{7,4},{8,9},{9,10},{10,1... | collective-permute-start | bytes 393224 | tf_op jit(solution)/shard_map/ppermute | solution.py:37
  7.4 8.4 %collective-permute-start.14 = (f32[1,32,256]{2,1,0:T(8,128)}, f32[1,32,256]{2,1,0:T(8,128)}, u32[]{:S(2)}, u32[]{:S(2)}) collective-permute-start(f32[1,32,256]{2,1,0:T(8,128)} %get-tuple-element.26), channel_id=1, source_target_pairs={{0,28},{4,0},{8,4},{12,8},{16,12},{20,16},{24,20},{28,24},{1,29},{... | collective-permute-start | bytes 98312 | tf_op jit(solution)/shard_map/ppermute | solution.py:21
  13.5 27.8 %copy-start.25 = (f32[2,2,8,8,1]{3,2,1,0,4:T(8,128)S(1)}, f32[2,2,8,8,1]{3,2,1,0,4:T(8,128)}, u32[]{:S(2)}) copy-start(f32[2,2,8,8,1]{3,2,1,0,4:T(8,128)} %constant.155) | copy-start | bytes 3076
  15.7 26.1 %copy-start.11 = (f32[2,8,256]{2,1,0:T(8,128)S(1)}, f32[2,8,256]{2,1,0:T(8,128)}, u32[]{:S(2)}) copy-start(f32[2,8,256]{2,1,0:T(8,128)} %constant.150.clone) | copy-start | bytes 49156
  15.7 26.1 %copy-start.15 = (f32[2,8,256]{2,1,0:T(8,128)S(1)}, f32[2,8,256]{2,1,0:T(8,128)}, u32[]{:S(2)}) copy-start(f32[2,8,256]{2,1,0:T(8,128)} %constant.151.clone) | copy-start | bytes 49156
  15.7 3.7 %collective-permute-start.15 = (f32[1,32,256]{2,1,0:T(8,128)}, f32[1,32,256]{2,1,0:T(8,128)S(1)}, u32[]{:S(2)}, u32[]{:S(2)}) collective-permute-start(f32[1,32,256]{2,1,0:T(8,128)} %get-tuple-element.25), channel_id=1, source_target_pairs={{0,24},{4,28},{8,0},{12,4},{16,8},{20,12},{24,16},{28,20},{1,25},{... | collective-permute-start | bytes 98312 | tf_op jit(solution)/shard_map/ppermute | solution.py:21
  19.4 4.9 %collective-permute-start.16 = (f32[1,32,256]{2,1,0:T(8,128)}, f32[1,32,256]{2,1,0:T(8,128)S(1)}, u32[]{:S(2)}, u32[]{:S(2)}) collective-permute-start(f32[1,32,256]{2,1,0:T(8,128)} %get-tuple-element.24), channel_id=1, source_target_pairs={{0,20},{4,24},{8,28},{12,0},{16,4},{20,8},{24,12},{28,16},{1,21},{... | collective-permute-start | bytes 98312 | tf_op jit(solution)/shard_map/ppermute | solution.py:21
  24.4 3.0 %collective-permute-start.17 = (f32[1,32,256]{2,1,0:T(8,128)}, f32[1,32,256]{2,1,0:T(8,128)S(1)}, u32[]{:S(2)}, u32[]{:S(2)}) collective-permute-start(f32[1,32,256]{2,1,0:T(8,128)} %get-tuple-element.23), channel_id=1, source_target_pairs={{0,16},{4,20},{8,24},{12,28},{16,0},{20,4},{24,8},{28,12},{1,17},{... | collective-permute-start | bytes 98312 | tf_op jit(solution)/shard_map/ppermute | solution.py:21
  27.3 6.1 %collective-permute-start.18 = (f32[1,32,256]{2,1,0:T(8,128)}, f32[1,32,256]{2,1,0:T(8,128)S(1)}, u32[]{:S(2)}, u32[]{:S(2)}) collective-permute-start(f32[1,32,256]{2,1,0:T(8,128)} %get-tuple-element.22), channel_id=1, source_target_pairs={{0,12},{4,16},{8,20},{12,24},{16,28},{20,0},{24,4},{28,8},{1,13},{... | collective-permute-start | bytes 98312 | tf_op jit(solution)/shard_map/ppermute | solution.py:21
  33.4 3.9 %collective-permute-start.19 = (f32[1,32,256]{2,1,0:T(8,128)}, f32[1,32,256]{2,1,0:T(8,128)S(1)}, u32[]{:S(2)}, u32[]{:S(2)}) collective-permute-start(f32[1,32,256]{2,1,0:T(8,128)} %get-tuple-element.21), channel_id=1, source_target_pairs={{0,8},{4,12},{8,16},{12,20},{16,24},{20,28},{24,0},{28,4},{1,9},{5... | collective-permute-start | bytes 98312 | tf_op jit(solution)/shard_map/ppermute | solution.py:21
  37.3 2.4 %collective-permute-start.20 = (f32[1,32,256]{2,1,0:T(8,128)}, f32[1,32,256]{2,1,0:T(8,128)S(1)}, u32[]{:S(2)}, u32[]{:S(2)}) collective-permute-start(f32[1,32,256]{2,1,0:T(8,128)} %get-tuple-element.20), channel_id=1, source_target_pairs={{0,4},{4,8},{8,12},{12,16},{16,20},{20,24},{24,28},{28,0},{1,5},{5... | collective-permute-start | bytes 98312 | tf_op jit(solution)/shard_map/ppermute | solution.py:21
  39.7 13.1 %collective-permute-start.6 = (bf16[256,256]{1,0:T(8,128)(2,1)}, bf16[256,256]{1,0:T(8,128)(2,1)S(1)}, u32[]{:S(2)}, u32[]{:S(2)}) collective-permute-start(bf16[256,256]{1,0:T(8,128)(2,1)} %param.12), channel_id=1, source_target_pairs={{0,3},{1,0},{2,1},{3,2},{4,7},{5,4},{6,5},{7,6},{8,11},{9,8},{10,9... | collective-permute-start | bytes 393224 | tf_op jit(solution)/shard_map/ppermute | solution.py:37
  42.7 10.3 %collective-permute-start.5 = (bf16[256,256]{1,0:T(8,128)(2,1)S(1)}, bf16[256,256]{1,0:T(8,128)(2,1)S(1)}, u32[]{:S(2)}, u32[]{:S(2)}) collective-permute-start(bf16[256,256]{1,0:T(8,128)(2,1)S(1)} %copy-done.14), channel_id=1, source_target_pairs={{0,2},{1,3},{2,0},{3,1},{4,6},{5,7},{6,4},{7,5},{8,10},{9,11},{10,... | collective-permute-start | bytes 393224 | tf_op jit(solution)/shard_map/ppermute | solution.py:37
  44.7 6.9 %copy-start.9 = (f32[256,256]{0,1:T(8,128)S(1)}, f32[256,256]{0,1:T(8,128)}, u32[]{:S(2)}) copy-start(f32[256,256]{0,1:T(8,128)} %fusion.98) | copy-start | bytes 786436
  47.2 6.2 %copy-start.17 = (f32[3,256]{1,0:T(4,128)S(1)}, f32[3,256]{1,0:T(4,128)}, u32[]{:S(2)}) copy-start(f32[3,256]{1,0:T(4,128)} %get-tuple-element.37) | copy-start | bytes 9220
  47.2 6.2 %copy-start.19 = (f32[3,256]{1,0:T(4,128)S(1)}, f32[3,256]{1,0:T(4,128)}, u32[]{:S(2)}) copy-start(f32[3,256]{1,0:T(4,128)} %get-tuple-element.38) | copy-start | bytes 9220
  47.2 6.2 %copy-start.21 = (f32[3,256]{1,0:T(4,128)S(1)}, f32[3,256]{1,0:T(4,128)}, u32[]{:S(2)}) copy-start(f32[3,256]{1,0:T(4,128)} %get-tuple-element.39) | copy-start | bytes 9220
  47.2 6.1 %collective-permute-start.3 = (bf16[3,2,256]{2,1,0:T(2,128)(2,1)S(1)}, bf16[3,2,256]{2,1,0:T(2,128)(2,1)S(1)}, u32[]{:S(2)}, u32[]{:S(2)}) collective-permute-start(bf16[3,2,256]{2,1,0:T(2,128)(2,1)S(1)} %slice.175), channel_id=1, source_target_pairs={{0,4},{4,8},{8,12},{12,16},{16,20},{20,24},{24,28},{1,5},{5,9},{9,... | collective-permute-start | bytes 9224 | tf_op jit(solution)/shard_map/ppermute | solution.py:29
  55.5 6.4 %collective-permute-start.7 = (bf16[2,32,256]{1,2,0:T(8,128)(2,1)}, bf16[2,32,256]{1,2,0:T(8,128)(2,1)}, u32[]{:S(2)}, u32[]{:S(2)}) collective-permute-start(bf16[2,32,256]{1,2,0:T(8,128)(2,1)} %get-tuple-element.36), channel_id=1, source_target_pairs={{0,28},{4,0},{8,4},{12,8},{16,12},{20,16},{24,20},{28,24},{1,29},{... | collective-permute-start | bytes 98312 | tf_op jit(solution)/shard_map/ppermute | solution.py:21
  57.7 41.0 %copy-start.10 = (bf16[2,32,256]{2,1,0:T(8,128)(2,1)S(1)}, bf16[2,32,256]{2,1,0:T(8,128)(2,1)}, u32[]{:S(2)}) copy-start(bf16[2,32,256]{2,1,0:T(8,128)(2,1)} %copy.39) | copy-start | bytes 98308
  57.7 29.2 %collective-permute-start.13 = (bf16[2,32,256]{1,2,0:T(8,128)(2,1)}, bf16[2,32,256]{1,2,0:T(8,128)(2,1)}, u32[]{:S(2)}, u32[]{:S(2)}) collective-permute-start(bf16[2,32,256]{1,2,0:T(8,128)(2,1)} %get-tuple-element.30), channel_id=1, source_target_pairs={{0,4},{4,8},{8,12},{12,16},{16,20},{20,24},{24,28},{28,0},{1,5},{5... | collective-permute-start | bytes 98312 | tf_op jit(solution)/shard_map/ppermute | solution.py:21
  59.4 24.5 %collective-permute-start.12 = (bf16[2,32,256]{1,2,0:T(8,128)(2,1)}, bf16[2,32,256]{1,2,0:T(8,128)(2,1)}, u32[]{:S(2)}, u32[]{:S(2)}) collective-permute-start(bf16[2,32,256]{1,2,0:T(8,128)(2,1)} %get-tuple-element.31), channel_id=1, source_target_pairs={{0,8},{4,12},{8,16},{12,20},{16,24},{20,28},{24,0},{28,4},{1,9},{5... | collective-permute-start | bytes 98312 | tf_op jit(solution)/shard_map/ppermute | solution.py:21
  61.9 19.0 %collective-permute-start.11 = (bf16[2,32,256]{1,2,0:T(8,128)(2,1)}, bf16[2,32,256]{1,2,0:T(8,128)(2,1)}, u32[]{:S(2)}, u32[]{:S(2)}) collective-permute-start(bf16[2,32,256]{1,2,0:T(8,128)(2,1)} %get-tuple-element.32), channel_id=1, source_target_pairs={{0,12},{4,16},{8,20},{12,24},{16,28},{20,0},{24,4},{28,8},{1,13},{... | collective-permute-start | bytes 98312 | tf_op jit(solution)/shard_map/ppermute | solution.py:21
  61.9 16.1 %collective-permute-start.10 = (bf16[2,32,256]{1,2,0:T(8,128)(2,1)}, bf16[2,32,256]{1,2,0:T(8,128)(2,1)}, u32[]{:S(2)}, u32[]{:S(2)}) collective-permute-start(bf16[2,32,256]{1,2,0:T(8,128)(2,1)} %get-tuple-element.33), channel_id=1, source_target_pairs={{0,16},{4,20},{8,24},{12,28},{16,0},{20,4},{24,8},{28,12},{1,17},{... | collective-permute-start | bytes 98312 | tf_op jit(solution)/shard_map/ppermute | solution.py:21
  61.9 9.4 %collective-permute-start.8 = (bf16[2,32,256]{1,2,0:T(8,128)(2,1)}, bf16[2,32,256]{1,2,0:T(8,128)(2,1)}, u32[]{:S(2)}, u32[]{:S(2)}) collective-permute-start(bf16[2,32,256]{1,2,0:T(8,128)(2,1)} %get-tuple-element.35), channel_id=1, source_target_pairs={{0,24},{4,28},{8,0},{12,4},{16,8},{20,12},{24,16},{28,20},{1,25},{... | collective-permute-start | bytes 98312 | tf_op jit(solution)/shard_map/ppermute | solution.py:21
  71.3 5.0 %collective-permute-start.9 = (bf16[2,32,256]{1,2,0:T(8,128)(2,1)}, bf16[2,32,256]{1,2,0:T(8,128)(2,1)}, u32[]{:S(2)}, u32[]{:S(2)}) collective-permute-start(bf16[2,32,256]{1,2,0:T(8,128)(2,1)} %get-tuple-element.34), channel_id=1, source_target_pairs={{0,20},{4,24},{8,28},{12,0},{16,4},{20,8},{24,12},{28,16},{1,21},{... | collective-permute-start | bytes 98312 | tf_op jit(solution)/shard_map/ppermute | solution.py:21
  88.5 13.2 %copy-start.16 = (f32[2,8,256]{2,1,0:T(8,128)S(1)}, f32[2,8,256]{2,1,0:T(8,128)}, u32[]{:S(2)}) copy-start(f32[2,8,256]{2,1,0:T(8,128)} %constant.151.clone) | copy-start | bytes 49156
  106.5 2.7 %copy-start.24 = (f32[2,8,256]{2,1,0:T(8,128)S(1)}, f32[2,8,256]{2,1,0:T(8,128)}, u32[]{:S(2)}) copy-start(f32[2,8,256]{2,1,0:T(8,128)} %constant.153) | copy-start | bytes 49156
  110.0 11.6 %copy-start.6 = (f32[256,256]{1,0:T(8,128)S(1)}, f32[256,256]{1,0:T(8,128)}, u32[]{:S(2)}) copy-start(f32[256,256]{1,0:T(8,128)} %copy-done.5) | copy-start | bytes 786436
  110.0 11.6 %copy-start.27 = (f32[256]{0:T(256)S(1)}, f32[256]{0:T(256)}, u32[]{:S(2)}) copy-start(f32[256]{0:T(256)} %param.15) | copy-start | bytes 3076
  122.6 7.9 %copy-start.18 = (f32[3,256]{1,0:T(4,128)S(1)}, f32[3,256]{1,0:T(4,128)}, u32[]{:S(2)}) copy-start(f32[3,256]{1,0:T(4,128)} %get-tuple-element.37) | copy-start | bytes 9220
  122.6 7.9 %copy-start.20 = (f32[3,256]{1,0:T(4,128)S(1)}, f32[3,256]{1,0:T(4,128)}, u32[]{:S(2)}) copy-start(f32[3,256]{1,0:T(4,128)} %get-tuple-element.38) | copy-start | bytes 9220
  122.6 7.9 %copy-start.22 = (f32[3,256]{1,0:T(4,128)S(1)}, f32[3,256]{1,0:T(4,128)}, u32[]{:S(2)}) copy-start(f32[3,256]{1,0:T(4,128)} %get-tuple-element.39) | copy-start | bytes 9220
  123.1 7.3 %collective-permute-start.24 = (f32[3,2,256]{2,1,0:T(2,128)S(1)}, f32[3,2,256]{2,1,0:T(2,128)S(1)}, u32[]{:S(2)}, u32[]{:S(2)}) collective-permute-start(f32[3,2,256]{2,1,0:T(2,128)S(1)} %slice.212), channel_id=1, source_target_pairs={{4,0},{8,4},{12,8},{16,12},{20,16},{24,20},{28,24},{5,1},{9,5},{13... | collective-permute-start | bytes 18440 | tf_op jit(solution)/shard_map/ppermute | solution.py:29
  126.4 11.6 %collective-permute-start.21 = (bf16[256,256]{1,0:T(8,128)(2,1)S(1)}, bf16[256,256]{1,0:T(8,128)(2,1)S(1)}, u32[]{:S(2)}, u32[]{:S(2)}) collective-permute-start(bf16[256,256]{1,0:T(8,128)(2,1)S(1)} %convolution_convert_fusion.2), channel_id=1, source_target_pairs={{0,1},{1,2},{2,3},{3,0},{4,5},{5,6},{6,7},{7,4},{8,9},{9,10},{10,1... | collective-permute-start | bytes 393224 | tf_op jit(solution)/shard_map/ppermute | solution.py:48
  129.1 17.4 %collective-permute-start.22 = (bf16[256,256]{1,0:T(8,128)(2,1)S(1)}, bf16[256,256]{1,0:T(8,128)(2,1)S(1)}, u32[]{:S(2)}, u32[]{:S(2)}) collective-permute-start(bf16[256,256]{1,0:T(8,128)(2,1)S(1)} %convolution_convert_fusion.1), channel_id=1, source_target_pairs={{0,2},{1,3},{2,0},{3,1},{4,6},{5,7},{6,4},{7,5},{8,10},{9,11},{10,... | collective-permute-start | bytes 393224 | tf_op jit(solution)/shard_map/ppermute | solution.py:48
  130.1 17.3 %collective-permute-start.23 = (bf16[256,256]{1,0:T(8,128)(2,1)S(1)}, bf16[256,256]{1,0:T(8,128)(2,1)S(1)}, u32[]{:S(2)}, u32[]{:S(2)}) collective-permute-start(bf16[256,256]{1,0:T(8,128)(2,1)S(1)} %convolution_convert_fusion), channel_id=1, source_target_pairs={{0,3},{1,0},{2,1},{3,2},{4,7},{5,4},{6,5},{7,6},{8,11},{9,8},{10,9... | collective-permute-start | bytes 393224 | tf_op jit(solution)/shard_map/ppermute | solution.py:48
  131.4 17.9 %collective-permute-start.25 = (bf16[256,256]{1,0:T(8,128)(2,1)S(1)}, bf16[256,256]{1,0:T(8,128)(2,1)S(1)}, u32[]{:S(2)}, u32[]{:S(2)}) collective-permute-start(bf16[256,256]{1,0:T(8,128)(2,1)S(1)} %fusion.30), channel_id=1, source_target_pairs={{0,1},{1,2},{2,3},{3,0},{4,5},{5,6},{6,7},{7,4},{8,9},{9,10},{10,1... | collective-permute-start | bytes 393224 | tf_op jit(solution)/shard_map/ppermute | solution.py:48
  132.6 19.4 %collective-permute-start.26 = (bf16[256,256]{1,0:T(8,128)(2,1)S(1)}, bf16[256,256]{1,0:T(8,128)(2,1)S(1)}, u32[]{:S(2)}, u32[]{:S(2)}) collective-permute-start(bf16[256,256]{1,0:T(8,128)(2,1)S(1)} %fusion.31), channel_id=1, source_target_pairs={{0,2},{1,3},{2,0},{3,1},{4,6},{5,7},{6,4},{7,5},{8,10},{9,11},{10,... | collective-permute-start | bytes 393224 | tf_op jit(solution)/shard_map/ppermute | solution.py:48
  138.1 15.0 %collective-permute-start.27 = (bf16[256,256]{1,0:T(8,128)(2,1)S(1)}, bf16[256,256]{1,0:T(8,128)(2,1)S(1)}, u32[]{:S(2)}, u32[]{:S(2)}) collective-permute-start(bf16[256,256]{1,0:T(8,128)(2,1)S(1)} %fusion.32), channel_id=1, source_target_pairs={{0,3},{1,0},{2,1},{3,2},{4,7},{5,4},{6,5},{7,6},{8,11},{9,8},{10,9... | collective-permute-start | bytes 393224 | tf_op jit(solution)/shard_map/ppermute | solution.py:48
  (8 other events, 9.3 us)
